TPU v7x, 32 devices: a whole 2x2x4 slice. The times are simulated.
32 devices in a mesh: seq: 8 (over z, x), ch: 4 (over y, core).
Axes of the slice: x: 2, y: 2, z: 4, core: 2. Of those that a mesh axis runs over, the one named last changes fastest.
Arguments:
- xin: bfloat16 [8192, 16384], P('seq', 'ch'), may hold values from -6 to 6
- gate_in: bfloat16 [8192, 16384], P('seq', 'ch'), may hold values from -6 to 6
- bc_proj: bfloat16 [8192, 256], P('seq', 'ch'), may hold values from -6 to 6
- dt_raw: float32 [8192, 128], P('seq', 'ch'), may hold values from -6 to 6
- dt_bias: float32 [128], P('ch'), may hold values from -1 to 1
- rate: float32 [128], P('ch'), may hold values from 6.1035156e-05 to 0.1
- skip_gain: float32 [128], P('ch'), may hold values from 0.5 to 2
- conv_x: bfloat16 [4, 16384], P(None, 'ch'), may hold values from -3 to 3
- conv_bc: bfloat16 [4, 256], P(None, 'ch'), may hold values from -3 to 3
- norm_gain: float32 [16384], P('ch'), may hold values from 0.5 to 1.5
- valid_blocks: int32 [8], P('seq'), may hold values from 1 to 8, 48 in all
Outputs:
- mixed: bfloat16 [8192, 16384], P('seq', 'ch')
Inputs may be any that keep to these rules, and one draw needn't show every extreme that they name: valid_blocks sums to 48; some entry equals 8.
All inputs are finite; a program needn't handle non-finite values.
Results may differ from a plain program's by a relative error of at most 0.0034.
Values may be sent and summed in bfloat16 or wider, within the bound.
No kernel may reach another device: no remote copies, remote signals or barrier semaphores. Data moves between devices by JAX's collectives and lax.ppermute only.
A program may use at most 256 MiB of HBM per device.

v0:
```python
import jax
import jax.numpy as jnp
from jax import lax
from jax.sharding import PartitionSpec as P

SEGMENT_LENGTH = 256
BLOCK = 128
INNER = 16384


def passed_along(block, axis, distance):
    devices = range(lax.axis_size(axis))
    route = [(i - distance, i) for i in devices if i - distance in devices]
    return lax.ppermute(block, axis, route)


def prefix(part, axis, combine, identity):
    place = lax.axis_index(axis)
    gathered = jax.tree.map(lambda a: lax.all_gather(a, axis), part)
    state = jax.tree.map(lambda a, e: jnp.zeros_like(a) + jnp.asarray(e, a.dtype), part, identity)

    def one(turn, state):
        return combine(
            state, jax.tree.map(lambda a: lax.dynamic_index_in_dim(a, turn, 0, False), gathered)
        )

    return lax.fori_loop(0, place, one, state)


def scan_states(factor, state, axis):
    count = lax.axis_size(axis)
    heads, size, width = state.shape
    piece = size // count
    parts = state.reshape(heads, count, piece, width).transpose(1, 0, 2, 3)
    got = lax.all_to_all(parts, axis, 0, 0, tiled=True)
    decays = lax.all_gather(factor, axis)
    running = jnp.zeros((heads, piece, width), jnp.float32)
    entries = []
    for index in range(count):
        entries.append(running)
        running = decays[index][:, None, None] * running + got[index]
    back = lax.all_to_all(jnp.stack(entries, axis=0), axis, 0, 0, tiled=True)
    return back.transpose(1, 0, 2, 3).reshape(heads, size, width)


def conv_silu(signal, tail_rows, weights):
    stacked = jnp.concatenate([tail_rows, signal], axis=0)
    kernel_taps = weights.shape[0]
    length = signal.shape[0]
    accum = jnp.zeros(signal.shape, jnp.float32)
    for offset in range(kernel_taps):
        accum = accum + weights[offset].astype(jnp.float32) * stacked[
            offset : offset + length
        ].astype(jnp.float32)
    return jax.nn.silu(accum).astype(jnp.bfloat16)


def combine_states(earlier, latter):
    return (earlier[0] * latter[0], latter[0][:, None, None] * earlier[1] + latter[1])


def local(
    xin,
    gate_in,
    bc_proj,
    dt_raw,
    dt_bias,
    rate,
    skip_gain,
    conv_x,
    conv_bc,
    norm_gain,
    valid_blocks,
):
    row_count, channels = xin.shape
    head_count = dt_raw.shape[1]
    head_size = channels // head_count
    span_count = row_count // SEGMENT_LENGTH
    kernel_taps = conv_x.shape[0]
    live_rows = valid_blocks[0] * BLOCK
    tail_x = lax.dynamic_slice_in_dim(xin, live_rows - (kernel_taps - 1), kernel_taps - 1, 0)
    tail_bc = lax.dynamic_slice_in_dim(bc_proj, live_rows - (kernel_taps - 1), kernel_taps - 1, 0)
    prev_x, prev_bc = passed_along((tail_x, tail_bc), "seq", 1)
    xconv = conv_silu(xin, prev_x, conv_x)
    bc_local = conv_silu(bc_proj, prev_bc, conv_bc)
    bc_full = lax.all_gather(bc_local, "ch", axis=1, tiled=True)
    state_size = bc_full.shape[1] // 2
    row_valid = (jnp.arange(row_count) < live_rows).astype(jnp.float32)
    step_size = jax.nn.softplus(dt_raw + dt_bias[None, :]) * row_valid[:, None]
    xfour = xconv.reshape(span_count, SEGMENT_LENGTH, head_count, head_size)
    b_three = bc_full[:, :state_size].reshape(span_count, SEGMENT_LENGTH, state_size)
    c_three = bc_full[:, state_size:].reshape(span_count, SEGMENT_LENGTH, state_size)
    step_three = step_size.reshape(span_count, SEGMENT_LENGTH, head_count)
    cumul = jnp.cumsum(-rate[None, None, :] * step_three, axis=1)
    scores = jnp.einsum("cqn,csn->cqs", c_three, b_three, preferred_element_type=jnp.float32)
    cum_heads = jnp.transpose(cumul, (0, 2, 1))
    diff = cum_heads[:, :, :, None] - cum_heads[:, :, None, :]
    causal = jnp.arange(SEGMENT_LENGTH)[:, None] >= jnp.arange(SEGMENT_LENGTH)[None, :]
    decay = jnp.where(causal, jnp.exp(jnp.where(causal, diff, 0.0)), 0.0)
    weights = (
        scores[:, None] * decay * jnp.transpose(step_three, (0, 2, 1))[:, :, None, :]
    ).astype(jnp.bfloat16)
    intra = jnp.einsum("chqs,cshp->cqhp", weights, xfour, preferred_element_type=jnp.float32)
    last_cum = cum_heads[:, :, -1]
    to_end = jnp.exp(last_cum[:, None, :] - cumul) * step_three
    x_weighted = (xfour.astype(jnp.float32) * to_end[..., None]).astype(jnp.bfloat16)
    block_state = jnp.einsum(
        "csn,cshp->chnp", b_three, x_weighted, preferred_element_type=jnp.float32
    )
    block_decay = jnp.exp(last_cum)
    current = jnp.zeros((head_count, state_size, head_size), jnp.float32)
    factor = jnp.ones((head_count,), jnp.float32)
    local_enter = []
    factor_list = []
    for index in range(span_count):
        local_enter.append(current)
        factor_list.append(factor)
        current = block_decay[index][:, None, None] * current + block_state[index]
        factor = factor * block_decay[index]
    group_state = scan_states(factor, current, "seq")
    state_enter = jnp.stack(
        [
            local_enter[index] + factor_list[index][:, None, None] * group_state
            for index in range(span_count)
        ],
        axis=0,
    )
    inter = jnp.einsum(
        "cqn,chnp->cqhp", c_three.astype(jnp.float32), state_enter, precision=lax.Precision.HIGHEST
    )
    inter = inter * jnp.exp(cumul)[..., None]
    y_full = intra + inter + skip_gain[None, None, :, None] * xfour.astype(jnp.float32)
    y_full = y_full.reshape(row_count, channels)
    gated = y_full * jax.nn.silu(gate_in.astype(jnp.float32))
    square_sum = lax.psum(jnp.sum(gated * gated, axis=1), "ch")
    mean_sq = square_sum / INNER
    normed = gated * lax.rsqrt(mean_sq + 1e-05)[:, None] * norm_gain[None, :] * row_valid[:, None]
    return normed.astype(jnp.bfloat16)


def solution(mesh):
    placed = (
        P("seq", "ch"),
        P("seq", "ch"),
        P("seq", "ch"),
        P("seq", "ch"),
        P("ch"),
        P("ch"),
        P("ch"),
        P(None, "ch"),
        P(None, "ch"),
        P("ch"),
        P("seq"),
    )
    return jax.shard_map(
        local, mesh=mesh, in_specs=placed, out_specs=P("seq", "ch"), check_vma=False
    )
```

profile of v0, /device:TPU:0, one launch (start us, length us, event | category | flops | bytes accessed | tf_op | source)
XLA Modules:
  0.0 295.1 jit_solution(8217255166965492911)
XLA Ops:
  0.7 0.8 constant_dynamic-slice_fusion
  1.5 4.9 %collective-permute-start.1 = (bf16[3,64]{0,1:T(8,128)(2,1)S(1)}, bf16[3,64]{0,1:T(8,128)(2,1)S(1)}, u32[]{:S(2)}, u32[]{:S(2)}) collective-permute-start(bf16[3,64]{0,1:T(8,128)(2,1)S(1)} %constant_dynamic-slice_fusion), channel_id=1, source_target_pairs={{0,4},{4,8},{8,12},{12,16},{16,20},{20,24},{24,28},{1,5},{5,9},{9,... | collective-permute-start | bytes 1160 | tf_op jit(solution)/shard_map/ppermute | solution.py:14
  6.3 0.9 constant_dynamic-slice_fusion.1
  7.2 3.5 %collective-permute-start = (bf16[3,4096]{1,0:T(4,128)(2,1)S(1)}, bf16[3,4096]{1,0:T(4,128)(2,1)S(1)}, u32[]{:S(2)}, u32[]{:S(2)}) collective-permute-start(bf16[3,4096]{1,0:T(4,128)(2,1)S(1)} %constant_dynamic-slice_fusion.1), channel_id=1, source_target_pairs={{0,4},{4,8},{8,12},{12,16},{16,20},{20,24},{24,28},{1,5},{5,9},{9,... | collective-permute-start | bytes 73736 | tf_op jit(solution)/shard_map/ppermute | solution.py:14
  10.7 1.1 fusion.38
  11.8 0.7 neg.21
  12.5 0.1 multiply_bitcast_fusion
  12.6 0.1 reshape.168
  12.7 2.3 reduce-window.6
  15.1 0.1 copy.56
  15.3 0.1 copy_bitcast_fusion
  15.4 0.2 slice_reduce_fusion
  15.7 0.1 bitcast_multiply_fusion
  15.8 1.0 slice_convert_fusion.3
  16.8 0.8 bitcast_convert_fusion.3
  17.7 1.5 multiply_convert_fusion.6
  19.2 7.2 %all_gather.7 = bf16[1024,256]{0,1:T(8,128)(2,1)S(1)} all-gather(bf16[1024,64]{0,1:T(8,128)(2,1)S(1)} %multiply_convert_fusion.6), channel_id=1, replica_groups=mesh['seq'=8,'ch'=4] {'ch'}, dimensions={1}, use_global_device_ids=true | all-gather | bytes 655360 | tf_op jit(solution)/shard_map/all_gather | solution.py:86
  26.5 0.2 copy.82
  26.6 18.8 %fusion.26 = bf16[128,8,32,128]{3,1,2,0:T(8,128)(2,1)} fusion(bf16[1024,4096]{1,0:T(8,128)(2,1)} %param.11, f32[4096]{0:T(1024)S(1)} %bitcast.133, bf16[3,4096]{1,0:T(4,128)(2,1)S(1)} %collective-permute-done, f32[4096]{0:T(1024)S(1)} %bitcast.134, f32[4096]{0:T(1024)S(1)} %bitcast.132, f32[4096]{0:T(1024)S(1)} %bitcast.131), kind=kLoop, calls=%fused_computation.37 | loop fusion | flops 104857600 | bytes 16867328
  45.5 9.4 %copy.84 = bf16[128,8,32,128]{3,2,1,0:T(8,128)(2,1)} copy(bf16[128,8,32,128]{3,1,2,0:T(8,128)(2,1)} %fusion.26) | data formatting | bytes 16777216
  54.9 13.7 %copy.60 = bf16[4,256,32,128]{1,3,2,0:T(8,128)(2,1)} copy(bf16[4,256,32,128]{3,2,1,0:T(8,128)(2,1)} %bitcast.118) | data formatting | bytes 16777216 | tf_op jit(solution)/shard_map/reshape | solution.py:90
  68.6 6.3 %fusion.27 = f32[4,32,128,128]{3,2,1,0:T(8,128)S(1)} fusion(bf16[4,256,128,1]{2,1,3,0:T(8,128)(2,1)S(1)} %bitcast.126, bf16[4,256,32,128]{1,3,2,0:T(8,128)(2,1)} %copy.60, f32[4,256,32]{1,2,0:T(8,128)S(1)} %copy.64), kind=kOutput, calls=%fused_computation.38 | convolution fusion | flops 1086324736 | bytes 17170432 | tf_op jit(solution)/shard_map/csn,cshp->chnp/dot_general | solution.py:107
  74.9 0.6 fusion.51
  75.5 2.6 copy-done
  78.1 2.0 fusion.30
  80.2 4.8 %all-to-all-start = ((f32[8,32,16,128]{3,2,1,0:T(8,128)}), f32[8,32,16,128]{3,2,1,0:T(8,128)S(1)}, u32[]{:S(2)}, u32[]{:S(2)}) async-start(f32[8,32,16,128]{3,2,1,0:T(8,128)} %fusion.30), calls=%async_computation | async-start | bytes 4194304 | tf_op jit(solution)/shard_map/all_to_all | solution.py:35
  85.0 50.3 %all-gather = f32[8,1,32]{2,1,0:T(1,128)S(1)} all-gather(f32[1,1,32]{2,1,0:T(1,128)S(1)} %get-tuple-element.35), channel_id=1, replica_groups=mesh['seq'=8,'ch'=4] {'seq'}, dimensions={0}, use_global_device_ids=true | all-gather | bytes 1152 | tf_op jit(solution)/shard_map/all_gather | solution.py:36
  135.2 0.8 broadcast_dynamic-update-slice_fusion
  136.0 0.8 fusion.35
  136.8 0.9 constant_dynamic-update-slice_fusion.2
  137.7 0.8 fusion.40
  138.5 0.8 constant_dynamic-update-slice_fusion.1
  139.3 0.8 fusion.41
  140.2 0.8 constant_dynamic-update-slice_fusion
  141.0 0.8 fusion.34
  141.8 10.2 %all-to-all-start.1 = ((f32[8,32,16,128]{3,2,1,0:T(8,128)}), f32[8,32,16,128]{3,2,1,0:T(8,128)S(1)}, u32[]{:S(2)}, u32[]{:S(2)}) async-start(f32[8,32,16,128]{3,2,1,0:T(8,128)} %fusion.34), calls=%async_computation.1 | async-start | bytes 4194304 | tf_op jit(solution)/shard_map/all_to_all | solution.py:42
  152.1 0.1 exponential_bitcast_fusion
  152.2 0.2 copy.52
  152.4 1.3 fusion.53
  153.7 44.1 %all-to-all-done.1 = f32[8,32,16,128]{3,2,1,0:T(8,128)S(1)} async-done(((f32[8,32,16,128]{3,2,1,0:T(8,128)}), f32[8,32,16,128]{3,2,1,0:T(8,128)S(1)}, u32[]{:S(2)}, u32[]{:S(2)}) %all-to-all-start.1) | async-done | bytes 2097184 | tf_op jit(solution)/shard_map/all_to_all | solution.py:42
  197.8 0.3 copy.71
  198.1 3.5 %multiply_add_fusion.1 = (f32[1,32,128,128]{3,2,1,0:T(8,128)S(1)}, f32[1,32,128,128]{3,2,1,0:T(8,128)S(1)}, f32[1,32,128,128]{3,2,1,0:T(8,128)S(1)}) fusion(f32[1,32,128,128]{3,2,1,0:T(8,128)S(1)} %bitcast.119, f32[32]{0:T(128)S(1)} %get-tuple-element.6, f32[4,32,128,128]{3,2,1,0:T(8,128)} %copy-done, f32[32]{0:T(128)S(1)} %get-tuple-element.38, ...), kind=kLoop, calls=%fused_computation.48 | loop fusion | flops 5767168 | bytes 14680832 | tf_op jit(solution)/shard_map/add | solution.py:123
  201.7 10.9 %fusion.17 = f32[4,256,32,128]{1,3,2,0:T(8,128)} fusion(bf16[4,256,128,1]{2,1,3,0:T(8,128)(2,1)S(1)} %bitcast.129, f32[1,32,128,128]{3,2,1,0:T(8,128)S(1)} %get-tuple-element.14, f32[1,32,128,128]{3,2,1,0:T(8,128)S(1)} %get-tuple-element.13, f32[1,32,128,128]{3,2,1,0:T(8,128)S(1)} %get-tuple-element.15, f32[1,32,128,128]{3,2,1,0:T(8,128)S(1)} %bitcast.120), kind=kOutput, calls=%fused_computation.28 | convolution fusion | flops 6448742400 | bytes 25427968 | tf_op jit(solution)/shard_map/cqn,chnp->cqhp/dot_general | solution.py:128
  212.6 16.9 %fusion.2 = f32[4,256,32,128]{1,3,2,0:T(8,128)} fusion(bf16[4,256,32,128]{1,3,2,0:T(8,128)(2,1)S(1)} %bitcast.117, f32[4,256,32,128]{1,3,2,0:T(8,128)} %fusion.17, f32[4,32,256]{2,1,0:T(8,128)S(1)} %copy.59, f32[4,32,256]{2,1,0:T(8,128)S(1)} %copy_bitcast_fusion, f32[4,256,256]{2,1,0:T(8,128)S(1)} %copy-done.1, pred[256,256]{1,0:T(8,128)(4,1)S(1)} %iota_compare_fusion, ...), kind=kOutput, calls=%fused_computation.7 | convolution fusion | flops 2218786816 | bytes 43450496 | tf_op jit(solution)/shard_map/chqs,cshp->cqhp/dot_general | solution.py:103
  229.6 19.9 %copy.73 = f32[4,256,32,128]{3,2,1,0:T(8,128)} copy(f32[4,256,32,128]{1,3,2,0:T(8,128)} %fusion.2) | data formatting | bytes 33554432 | tf_op jit(solution)/shard_map/add | solution.py:132
  249.4 16.2 %multiply_reduce_fusion = f32[1024]{0:T(1024)S(1)} fusion(bf16[1024,4096]{1,0:T(8,128)(2,1)} %param.12, f32[128,8,32,128]{3,2,1,0:T(8,128)} %bitcast.114), kind=kLoop, calls=%fused_computation.14 | loop fusion | flops 33553408 | bytes 25169920 | tf_op jit(solution)/shard_map/reduce_sum | solution.py:135
  265.6 5.7 %psum.7 = f32[1024]{0:T(1024)S(1)} all-reduce(f32[1024]{0:T(1024)S(1)} %multiply_reduce_fusion), channel_id=1, replica_groups=mesh['seq'=8,'ch'=4] {'ch'}, use_global_device_ids=true, to_apply=%region_3.4 | all-reduce | flops 1024 | bytes 8192 | tf_op jit(solution)/shard_map/psum | solution.py:135
  271.3 23.8 %multiply_convert_fusion.2 = bf16[1024,4096]{1,0:T(8,128)(2,1)} fusion(f32[1024]{0:T(1024)S(1)} %fusion.44, f32[4096]{0:T(1024)S(1)} %copy-done.2, f32[1024]{0:T(1024)S(1)} %add_rsqrt_fusion, bf16[1024,4096]{1,0:T(8,128)(2,1)} %param.12, f32[128,8,32,128]{3,2,1,0:T(8,128)} %bitcast.115), kind=kLoop, calls=%fused_computation.13 | loop fusion | flops 41943040 | bytes 33579008 | tf_op jit(solution)/shard_map/convert_element_type | solution.py:138
  (32 shorter events, 0.5 us)
Async XLA Ops:
  1.5 16.2 %collective-permute-start.1 = (bf16[3,64]{0,1:T(8,128)(2,1)S(1)}, bf16[3,64]{0,1:T(8,128)(2,1)S(1)}, u32[]{:S(2)}, u32[]{:S(2)}) collective-permute-start(bf16[3,64]{0,1:T(8,128)(2,1)S(1)} %constant_dynamic-slice_fusion), channel_id=1, source_target_pairs={{0,4},{4,8},{8,12},{12,16},{16,20},{20,24},{24,28},{1,5},{5,9},{9,... | collective-permute-start | bytes 1160 | tf_op jit(solution)/shard_map/ppermute | solution.py:14
  7.2 19.4 %collective-permute-start = (bf16[3,4096]{1,0:T(4,128)(2,1)S(1)}, bf16[3,4096]{1,0:T(4,128)(2,1)S(1)}, u32[]{:S(2)}, u32[]{:S(2)}) collective-permute-start(bf16[3,4096]{1,0:T(4,128)(2,1)S(1)} %constant_dynamic-slice_fusion.1), channel_id=1, source_target_pairs={{0,4},{4,8},{8,12},{12,16},{16,20},{20,24},{24,28},{1,5},{5,9},{9,... | collective-permute-start | bytes 73736 | tf_op jit(solution)/shard_map/ppermute | solution.py:14
  74.9 3.2 %copy-start = (f32[4,32,128,128]{3,2,1,0:T(8,128)}, f32[4,32,128,128]{3,2,1,0:T(8,128)S(1)}, u32[]{:S(2)}) copy-start(f32[4,32,128,128]{3,2,1,0:T(8,128)S(1)} %fusion.27) | copy-start | bytes 25165828
  80.2 55.9 %all-to-all-start = ((f32[8,32,16,128]{3,2,1,0:T(8,128)}), f32[8,32,16,128]{3,2,1,0:T(8,128)S(1)}, u32[]{:S(2)}, u32[]{:S(2)}) async-start(f32[8,32,16,128]{3,2,1,0:T(8,128)} %fusion.30), calls=%async_computation | async-start | bytes 4194304 | tf_op jit(solution)/shard_map/all_to_all | solution.py:35
  141.8 56.0 %all-to-all-start.1 = ((f32[8,32,16,128]{3,2,1,0:T(8,128)}), f32[8,32,16,128]{3,2,1,0:T(8,128)S(1)}, u32[]{:S(2)}, u32[]{:S(2)}) async-start(f32[8,32,16,128]{3,2,1,0:T(8,128)} %fusion.34), calls=%async_computation.1 | async-start | bytes 4194304 | tf_op jit(solution)/shard_map/all_to_all | solution.py:42
  198.1 14.5 %slice-start = ((s8[8388608]{0:T(1024)(128)(4,1)}), s8[4194304]{0:T(1024)(128)(4,1)S(1)}, s32[]{:S(2)}) async-start(s8[8388608]{0:T(1024)(128)(4,1)} %bitcast.116), calls=%async_computation.2 | async-start | bytes 8388608
  201.6 11.0 %slice-start.1 = ((s8[8388608]{0:T(1024)(128)(4,1)}), s8[4194304]{0:T(1024)(128)(4,1)S(1)}, s32[]{:S(2)}) async-start(s8[8388608]{0:T(1024)(128)(4,1)} %bitcast.116), calls=%async_computation.3 | async-start | bytes 8388608
  201.7 11.0 %copy-start.1 = (f32[4,256,256]{2,1,0:T(8,128)S(1)}, f32[4,256,256]{2,1,0:T(8,128)}, u32[]{:S(2)}) copy-start(f32[4,256,256]{2,1,0:T(8,128)} %fusion.53) | copy-start | bytes 3145732
  201.7 11.0 %copy-start.3 = (f32[32]{0:T(128)S(1)}, f32[32]{0:T(128)}, u32[]{:S(2)}) copy-start(f32[32]{0:T(128)} %param.17) | copy-start | bytes 388
  249.4 21.9 %copy-start.2 = (f32[4096]{0:T(1024)S(1)}, f32[4096]{0:T(1024)}, u32[]{:S(2)}) copy-start(f32[4096]{0:T(1024)} %param.20) | copy-start | bytes 49156
where the time goes:
time: 296 us; the launch traced here: 295 us
  other arithmetic  78.1 us (26%)
  blocking collectives  63.2 us (21%)
  local copies, waits for them, and re-layouts  50 us (17%)
  waiting for transfers between devices  44.1 us (15%)
  matrix products  35.5 us (12%)
  starting transfers between devices  23.3 us (8%)
    all_gather x1, blocking collectives, scan_states(): decays = lax.all_gather(factor, axis)  50.3 us
    all_to_all x1, waiting for transfers between devices, scan_states(): back = lax.all_to_all(jnp.stack(entries, axis=0), axis, 0, 0, tiled=True)  44.1 us
    unnamed x8, other arithmetic  23.8 us
    convert_element_type x1, other arithmetic, local(): return normed.astype(jnp.bfloat16)  23.8 us
    add x1, local copies, waits for them, and re-layouts, local(): intra + inter + skip_gain[None, None, :, None] * xfour.astype(jnp.float32)  19.9 us
    dot_general x1, matrix products, local(): jnp.einsum('chqs,cshp->cqhp', weights, xfour, preferred_element_type=jnp....  16.9 us
    reduce_sum x1, other arithmetic, local(): square_sum = lax.psum(jnp.sum(gated * gated, axis=1), 'ch')  16.2 us
    reshape x1, local copies, waits for them, and re-layouts, local(): xfour = xconv.reshape(span_count, SEGMENT_LENGTH, head_count, head_size)  13.7 us
  transfers between devices with their start and end apart: 4, of which 1 were waited for; matrix products, arithmetic and copies ran while one was open for 4% of the time, Pallas kernels for 0%

commit v1 on v0

--- a/solution.py
+++ b/solution.py
@@ -6,6 +6,19 @@
 SEGMENT_LENGTH = 256
 BLOCK = 128
 INNER = 16384
+
+
+def ring_gather(value, axis, dim):
+    ways = lax.axis_size(axis)
+    up = [(d, (d + 1) % ways) for d in range(ways)]
+    down = [(d, (d - 1) % ways) for d in range(ways)]
+    earlier, later = ([value], [value])
+    for _ in range(ways // 2):
+        earlier.append(lax.ppermute(earlier[-1], axis, up))
+    for _ in range((ways - 1) // 2):
+        later.append(lax.ppermute(later[-1], axis, down))
+    line = jnp.concatenate([*earlier[::-1], *later[1:]], axis=dim)
+    return jnp.roll(line, (lax.axis_index(axis) - ways // 2) * value.shape[dim], axis=dim)
 
 
 def passed_along(block, axis, distance):
@@ -83,7 +96,7 @@
     prev_x, prev_bc = passed_along((tail_x, tail_bc), "seq", 1)
     xconv = conv_silu(xin, prev_x, conv_x)
     bc_local = conv_silu(bc_proj, prev_bc, conv_bc)
-    bc_full = lax.all_gather(bc_local, "ch", axis=1, tiled=True)
+    bc_full = ring_gather(bc_local, "ch", 1)
     state_size = bc_full.shape[1] // 2
     row_valid = (jnp.arange(row_count) < live_rows).astype(jnp.float32)
     step_size = jax.nn.softplus(dt_raw + dt_bias[None, :]) * row_valid[:, None]

time: 296 us -> 296 us (level)
  blocking collectives: 63.2 us -> 55.8 us
  waiting for transfers between devices: 44.1 us -> 47.3 us
    all_gather x1 -> x0, blocking collectives: 7.2 us -> none  [local(): bc_full = lax.all_gather(bc_local, 'ch', axis=1, tiled=True)]
    unnamed x15 -> x21, local copies, waits for them, and re-layouts: 13 us -> 12.9 us
  transfers between devices with their start and end apart: 4 -> 7, of which waited for: 1 -> 2; matrix products, arithmetic and copies ran while one was open for 4% -> 18% of each run, Pallas kernels for 0% -> 0%
where the time goes in v1:
time: 296 us; the launch traced here: 294 us
  other arithmetic  78.1 us (26%)
  blocking collectives  55.8 us (19%)
  local copies, waits for them, and re-layouts  50.2 us (17%)
  waiting for transfers between devices  47.3 us (16%)
  matrix products  35.5 us (12%)
  starting transfers between devices  26.2 us (9%)
    all_gather x1, blocking collectives, scan_states(): decays = lax.all_gather(factor, axis)  50 us
    all_to_all x1, waiting for transfers between devices, scan_states(): back = lax.all_to_all(jnp.stack(entries, axis=0), axis, 0, 0, tiled=True)  44.7 us
    unnamed x8, other arithmetic  23.8 us
    convert_element_type x1, other arithmetic, local(): return normed.astype(jnp.bfloat16)  23.8 us
    add x1, local copies, waits for them, and re-layouts, local(): intra + inter + skip_gain[None, None, :, None] * xfour.astype(jnp.float32)  19.9 us
    dot_general x1, matrix products, local(): jnp.einsum('chqs,cshp->cqhp', weights, xfour, preferred_element_type=jnp....  16.9 us
    reduce_sum x1, other arithmetic, local(): square_sum = lax.psum(jnp.sum(gated * gated, axis=1), 'ch')  16.2 us
    reshape x1, local copies, waits for them, and re-layouts, local(): xfour = xconv.reshape(span_count, SEGMENT_LENGTH, head_count, head_size)  13.7 us
  transfers between devices with their start and end apart: 7, of which 2 were waited for; matrix products, arithmetic and copies ran while one was open for 18% of the time, Pallas kernels for 0%

profile of v1, /device:TPU:0, one launch (start us, length us, event | category | flops | bytes accessed | tf_op | source)
XLA Modules:
  0.0 294.1 jit_solution(8197544129669939528)
XLA Ops:
  0.7 0.8 constant_dynamic-slice_fusion.2
  1.5 4.9 %collective-permute-start.1 = (bf16[3,64]{0,1:T(8,128)(2,1)S(1)}, bf16[3,64]{0,1:T(8,128)(2,1)S(1)}, u32[]{:S(2)}, u32[]{:S(2)}) collective-permute-start(bf16[3,64]{0,1:T(8,128)(2,1)S(1)} %constant_dynamic-slice_fusion.2), channel_id=1, source_target_pairs={{0,4},{4,8},{8,12},{12,16},{16,20},{20,24},{24,28},{1,5},{5,9},{9,... | collective-permute-start | bytes 1160 | tf_op jit(solution)/shard_map/ppermute | solution.py:27
  6.3 0.9 constant_dynamic-slice_fusion.3
  7.2 3.5 %collective-permute-start = (bf16[3,4096]{1,0:T(4,128)(2,1)S(1)}, bf16[3,4096]{1,0:T(4,128)(2,1)S(1)}, u32[]{:S(2)}, u32[]{:S(2)}) collective-permute-start(bf16[3,4096]{1,0:T(4,128)(2,1)S(1)} %constant_dynamic-slice_fusion.3), channel_id=1, source_target_pairs={{0,4},{4,8},{8,12},{12,16},{16,20},{20,24},{24,28},{1,5},{5,9},{9,... | collective-permute-start | bytes 73736 | tf_op jit(solution)/shard_map/ppermute | solution.py:27
  10.7 1.1 fusion.42
  11.8 0.7 neg.21
  12.7 2.3 reduce-window.6
  15.1 0.1 copy.79
  15.3 0.1 copy_bitcast_fusion
  15.4 0.2 slice_reduce_fusion
  15.7 0.1 bitcast_multiply_fusion
  15.8 1.0 slice_convert_fusion.3
  16.8 0.8 bitcast_convert_fusion.3
  17.6 1.5 multiply_convert_fusion.6
  19.3 1.7 collective-permute-start.4
  21.1 2.6 collective-permute-done.2
  23.6 18.8 %fusion.26 = bf16[128,8,32,128]{3,1,2,0:T(8,128)(2,1)} fusion(bf16[1024,4096]{1,0:T(8,128)(2,1)} %param.11, f32[4096]{0:T(1024)S(1)} %bitcast.133, bf16[3,4096]{1,0:T(4,128)(2,1)S(1)} %collective-permute-done, f32[4096]{0:T(1024)S(1)} %bitcast.134, f32[4096]{0:T(1024)S(1)} %bitcast.132, f32[4096]{0:T(1024)S(1)} %bitcast.131), kind=kLoop, calls=%fused_computation.37 | loop fusion | flops 104857600 | bytes 16867328
  42.5 9.4 %copy.110 = bf16[128,8,32,128]{3,2,1,0:T(8,128)(2,1)} copy(bf16[128,8,32,128]{3,1,2,0:T(8,128)(2,1)} %fusion.26) | data formatting | bytes 16777216
  51.9 13.7 %copy.83 = bf16[4,256,32,128]{1,3,2,0:T(8,128)(2,1)} copy(bf16[4,256,32,128]{3,2,1,0:T(8,128)(2,1)} %bitcast.118) | data formatting | bytes 16777216 | tf_op jit(solution)/shard_map/reshape | solution.py:103
  65.8 0.1 constant_dynamic-slice_fusion
  65.9 0.2 copy.75
  66.1 6.3 %fusion.27 = f32[4,32,128,128]{3,2,1,0:T(8,128)S(1)} fusion(bf16[4,256,128,1]{2,1,3,0:T(8,128)(2,1)S(1)} %bitcast.126, bf16[4,256,32,128]{1,3,2,0:T(8,128)(2,1)} %copy.83, f32[4,256,32]{1,2,0:T(8,128)S(1)} %copy.87), kind=kOutput, calls=%fused_computation.38 | convolution fusion | flops 1086324736 | bytes 17170432 | tf_op jit(solution)/shard_map/csn,cshp->chnp/dot_general | solution.py:120
  72.4 0.6 fusion.53
  73.0 2.6 copy-done
  75.6 2.0 fusion.30
  77.6 4.8 %all-to-all-start = ((f32[8,32,16,128]{3,2,1,0:T(8,128)}), f32[8,32,16,128]{3,2,1,0:T(8,128)S(1)}, u32[]{:S(2)}, u32[]{:S(2)}) async-start(f32[8,32,16,128]{3,2,1,0:T(8,128)} %fusion.30), calls=%async_computation | async-start | bytes 4194304 | tf_op jit(solution)/shard_map/all_to_all | solution.py:48
  82.4 50.0 %all-gather = f32[8,1,32]{2,1,0:T(1,128)S(1)} all-gather(f32[1,1,32]{2,1,0:T(1,128)S(1)} %get-tuple-element.35), channel_id=1, replica_groups=mesh['seq'=8,'ch'=4] {'seq'}, dimensions={0}, use_global_device_ids=true | all-gather | bytes 1152 | tf_op jit(solution)/shard_map/all_gather | solution.py:49
  132.4 0.7 broadcast_dynamic-update-slice_fusion
  133.2 0.8 fusion.39
  134.0 0.9 constant_dynamic-update-slice_fusion.12
  134.9 0.8 constant_dynamic-update-slice_fusion.11
  135.7 0.8 constant_dynamic-update-slice_fusion.10
  136.6 0.8 constant_dynamic-update-slice_fusion.9
  137.4 0.8 constant_dynamic-update-slice_fusion.8
  138.2 0.8 fusion.37
  139.0 11.3 %all-to-all-start.1 = ((f32[8,32,16,128]{3,2,1,0:T(8,128)}), f32[8,32,16,128]{3,2,1,0:T(8,128)S(1)}, u32[]{:S(2)}, u32[]{:S(2)}) async-start(f32[8,32,16,128]{3,2,1,0:T(8,128)} %fusion.37), calls=%async_computation.1 | async-start | bytes 4194304 | tf_op jit(solution)/shard_map/all_to_all | solution.py:55
  150.4 0.1 exponential_bitcast_fusion
  150.5 0.2 reshape.134
  150.7 1.3 fusion.34
  152.0 44.7 %all-to-all-done.1 = f32[8,32,16,128]{3,2,1,0:T(8,128)S(1)} async-done(((f32[8,32,16,128]{3,2,1,0:T(8,128)}), f32[8,32,16,128]{3,2,1,0:T(8,128)S(1)}, u32[]{:S(2)}, u32[]{:S(2)}) %all-to-all-start.1) | async-done | bytes 2097184 | tf_op jit(solution)/shard_map/all_to_all | solution.py:55
  196.8 0.3 copy.94
  197.0 3.5 %multiply_add_fusion.1 = (f32[1,32,128,128]{3,2,1,0:T(8,128)S(1)}, f32[1,32,128,128]{3,2,1,0:T(8,128)S(1)}, f32[1,32,128,128]{3,2,1,0:T(8,128)S(1)}) fusion(f32[1,32,128,128]{3,2,1,0:T(8,128)S(1)} %bitcast.119, f32[32]{0:T(128)S(1)} %get-tuple-element.6, f32[4,32,128,128]{3,2,1,0:T(8,128)} %copy-done, f32[32]{0:T(128)S(1)} %get-tuple-element.38, ...), kind=kLoop, calls=%fused_computation.48 | loop fusion | flops 5767168 | bytes 14680832 | tf_op jit(solution)/shard_map/add | solution.py:136
  200.6 10.9 %fusion.17 = f32[4,256,32,128]{1,3,2,0:T(8,128)} fusion(f32[1,32,128,128]{3,2,1,0:T(8,128)S(1)} %get-tuple-element.14, f32[1,32,128,128]{3,2,1,0:T(8,128)S(1)} %get-tuple-element.13, f32[1,32,128,128]{3,2,1,0:T(8,128)S(1)} %get-tuple-element.15, f32[1,32,128,128]{3,2,1,0:T(8,128)S(1)} %bitcast.120, bf16[4,256,128,1]{1,0,2,3:T(4,128)(2,1)S(1)} %bitcast.130), kind=kOutput, calls=%fused_computation.28 | convolution fusion | flops 6448742400 | bytes 25427968 | tf_op jit(solution)/shard_map/cqn,chnp->cqhp/dot_general | solution.py:141
  211.6 16.9 %fusion.2 = f32[4,256,32,128]{1,3,2,0:T(8,128)} fusion(bf16[4,256,32,128]{1,3,2,0:T(8,128)(2,1)S(1)} %bitcast.117, f32[4,256,32,128]{1,3,2,0:T(8,128)} %fusion.17, f32[4,32,256]{2,1,0:T(8,128)S(1)} %copy.82, f32[4,32,256]{2,1,0:T(8,128)S(1)} %copy_bitcast_fusion, f32[4,256,256]{2,1,0:T(8,128)S(1)} %copy-done.1, pred[256,256]{1,0:T(8,128)(4,1)S(1)} %iota_compare_fusion, ...), kind=kOutput, calls=%fused_computation.7 | convolution fusion | flops 2218786816 | bytes 43450496 | tf_op jit(solution)/shard_map/chqs,cshp->cqhp/dot_general | solution.py:116
  228.5 19.9 %copy.97 = f32[4,256,32,128]{3,2,1,0:T(8,128)} copy(f32[4,256,32,128]{1,3,2,0:T(8,128)} %fusion.2) | data formatting | bytes 33554432 | tf_op jit(solution)/shard_map/add | solution.py:145
  248.4 16.2 %multiply_reduce_fusion = f32[1024]{0:T(1024)S(1)} fusion(bf16[1024,4096]{1,0:T(8,128)(2,1)} %param.12, f32[128,8,32,128]{3,2,1,0:T(8,128)} %bitcast.114), kind=kLoop, calls=%fused_computation.14 | loop fusion | flops 33553408 | bytes 25169920 | tf_op jit(solution)/shard_map/reduce_sum | solution.py:148
  264.6 5.8 %psum.7 = f32[1024]{0:T(1024)S(1)} all-reduce(f32[1024]{0:T(1024)S(1)} %multiply_reduce_fusion), channel_id=1, replica_groups=mesh['seq'=8,'ch'=4] {'ch'}, use_global_device_ids=true, to_apply=%region_3.4 | all-reduce | flops 1024 | bytes 8192 | tf_op jit(solution)/shard_map/psum | solution.py:148
  270.4 23.8 %multiply_convert_fusion.2 = bf16[1024,4096]{1,0:T(8,128)(2,1)} fusion(f32[1024]{0:T(1024)S(1)} %fusion.46, f32[4096]{0:T(1024)S(1)} %copy-done.2, f32[1024]{0:T(1024)S(1)} %add_rsqrt_fusion, bf16[1024,4096]{1,0:T(8,128)(2,1)} %param.12, f32[128,8,32,128]{3,2,1,0:T(8,128)} %bitcast.115), kind=kLoop, calls=%fused_computation.13 | loop fusion | flops 41943040 | bytes 33579008 | tf_op jit(solution)/shard_map/convert_element_type | solution.py:151
  (45 shorter events, 0.8 us)
Async XLA Ops:
  1.5 16.2 %collective-permute-start.1 = (bf16[3,64]{0,1:T(8,128)(2,1)S(1)}, bf16[3,64]{0,1:T(8,128)(2,1)S(1)}, u32[]{:S(2)}, u32[]{:S(2)}) collective-permute-start(bf16[3,64]{0,1:T(8,128)(2,1)S(1)} %constant_dynamic-slice_fusion.2), channel_id=1, source_target_pairs={{0,4},{4,8},{8,12},{12,16},{16,20},{20,24},{24,28},{1,5},{5,9},{9,... | collective-permute-start | bytes 1160 | tf_op jit(solution)/shard_map/ppermute | solution.py:27
  7.2 16.4 %collective-permute-start = (bf16[3,4096]{1,0:T(4,128)(2,1)S(1)}, bf16[3,4096]{1,0:T(4,128)(2,1)S(1)}, u32[]{:S(2)}, u32[]{:S(2)}) collective-permute-start(bf16[3,4096]{1,0:T(4,128)(2,1)S(1)} %constant_dynamic-slice_fusion.3), channel_id=1, source_target_pairs={{0,4},{4,8},{8,12},{12,16},{16,20},{20,24},{24,28},{1,5},{5,9},{9,... | collective-permute-start | bytes 73736 | tf_op jit(solution)/shard_map/ppermute | solution.py:27
  19.2 4.4 %collective-permute-start.2 = (bf16[1024,64]{0,1:T(8,128)(2,1)S(1)}, bf16[1024,64]{0,1:T(8,128)(2,1)S(1)}, u32[]{:S(2)}, u32[]{:S(2)}) collective-permute-start(bf16[1024,64]{0,1:T(8,128)(2,1)S(1)} %multiply_convert_fusion.6), channel_id=1, source_target_pairs={{0,1},{1,2},{2,3},{3,0},{4,5},{5,6},{6,7},{7,4},{8,9},{9,10},{10,1... | collective-permute-start | bytes 393224 | tf_op jit(solution)/shard_map/ppermute | solution.py:17
  19.3 46.3 %collective-permute-start.4 = (bf16[1024,64]{0,1:T(8,128)(2,1)S(1)}, bf16[1024,64]{0,1:T(8,128)(2,1)S(1)}, u32[]{:S(2)}, u32[]{:S(2)}) collective-permute-start(bf16[1024,64]{0,1:T(8,128)(2,1)S(1)} %multiply_convert_fusion.6), channel_id=1, source_target_pairs={{0,3},{1,0},{2,1},{3,2},{4,7},{5,4},{6,5},{7,6},{8,11},{9,8},{10,9... | collective-permute-start | bytes 393224 | tf_op jit(solution)/shard_map/ppermute | solution.py:19
  23.6 42.0 %collective-permute-start.3 = (bf16[1024,64]{0,1:T(8,128)(2,1)S(1)}, bf16[1024,64]{0,1:T(8,128)(2,1)S(1)}, u32[]{:S(2)}, u32[]{:S(2)}) collective-permute-start(bf16[1024,64]{0,1:T(8,128)(2,1)S(1)} %collective-permute-done.2), channel_id=1, source_target_pairs={{0,1},{1,2},{2,3},{3,0},{4,5},{5,6},{6,7},{7,4},{8,9},{9,10},{10,1... | collective-permute-start | bytes 393224 | tf_op jit(solution)/shard_map/ppermute | solution.py:17
  72.4 3.2 %copy-start = (f32[4,32,128,128]{3,2,1,0:T(8,128)}, f32[4,32,128,128]{3,2,1,0:T(8,128)S(1)}, u32[]{:S(2)}) copy-start(f32[4,32,128,128]{3,2,1,0:T(8,128)S(1)} %fusion.27) | copy-start | bytes 25165828
  77.6 55.6 %all-to-all-start = ((f32[8,32,16,128]{3,2,1,0:T(8,128)}), f32[8,32,16,128]{3,2,1,0:T(8,128)S(1)}, u32[]{:S(2)}, u32[]{:S(2)}) async-start(f32[8,32,16,128]{3,2,1,0:T(8,128)} %fusion.30), calls=%async_computation | async-start | bytes 4194304 | tf_op jit(solution)/shard_map/all_to_all | solution.py:48
  139.0 57.7 %all-to-all-start.1 = ((f32[8,32,16,128]{3,2,1,0:T(8,128)}), f32[8,32,16,128]{3,2,1,0:T(8,128)S(1)}, u32[]{:S(2)}, u32[]{:S(2)}) async-start(f32[8,32,16,128]{3,2,1,0:T(8,128)} %fusion.37), calls=%async_computation.1 | async-start | bytes 4194304 | tf_op jit(solution)/shard_map/all_to_all | solution.py:55
  197.0 14.5 %slice-start = ((s8[8388608]{0:T(1024)(128)(4,1)}), s8[4194304]{0:T(1024)(128)(4,1)S(1)}, s32[]{:S(2)}) async-start(s8[8388608]{0:T(1024)(128)(4,1)} %bitcast.116), calls=%async_computation.2 | async-start | bytes 8388608
  200.6 11.0 %slice-start.1 = ((s8[8388608]{0:T(1024)(128)(4,1)}), s8[4194304]{0:T(1024)(128)(4,1)S(1)}, s32[]{:S(2)}) async-start(s8[8388608]{0:T(1024)(128)(4,1)} %bitcast.116), calls=%async_computation.3 | async-start | bytes 8388608
  200.6 11.0 %copy-start.1 = (f32[4,256,256]{2,1,0:T(8,128)S(1)}, f32[4,256,256]{2,1,0:T(8,128)}, u32[]{:S(2)}) copy-start(f32[4,256,256]{2,1,0:T(8,128)} %fusion.34) | copy-start | bytes 3145732
  200.6 11.0 %copy-start.3 = (f32[32]{0:T(128)S(1)}, f32[32]{0:T(128)}, u32[]{:S(2)}) copy-start(f32[32]{0:T(128)} %param.17) | copy-start | bytes 388
  248.4 22.0 %copy-start.2 = (f32[4096]{0:T(1024)S(1)}, f32[4096]{0:T(1024)}, u32[]{:S(2)}) copy-start(f32[4096]{0:T(1024)} %param.20) | copy-start | bytes 49156
